TPU v7x, 128 devices: a whole 4x4x4 slice. The times are simulated.
128 devices in a mesh: ctx: 8 (over x, core), tp: 8 (over z_hi, y), dp: 2 (over z_lo).
Axes of the slice: x: 4, y: 4, z: 4 (z_hi: 2, z_lo: 2; z = z_hi * 2 + z_lo), core: 2. Of those that a mesh axis runs over, the one named last changes fastest.
Arguments:
- activations: bfloat16 [16384, 4096], P(('ctx', 'tp', 'dp')), may hold values from -6 to 6
- out_grad: bfloat16 [16384, 4096], P(('ctx', 'tp', 'dp')), may hold values from -6 to 6
- routes: int32 [16384, 8], P(('ctx', 'tp', 'dp')), may hold values from 0 to 127, all different within a row; in each aligned block of 128 rows (0 to 127, 128 to 255, ...) at most 12 rows name the same one
- gate_probs: bfloat16 [16384, 8], P(('ctx', 'tp', 'dp')), may hold values from 0.049804688 to 0.59765625
- saved_pre: bfloat16 [64, 2, 768, 1536], P(('ctx', 'tp'), 'dp'), may hold values from -6 to 6
- expert_weights: bfloat16 [64, 4096, 2304], P(('ctx', 'tp'), 'dp'), may hold values from -0.09375 to 0.09375
Outputs:
- input_grad: bfloat16 [16384, 4096], P(('ctx', 'tp', 'dp'))
- prob_grad: bfloat16 [16384, 8], P(('ctx', 'tp', 'dp'))
- weight_grad: bfloat16 [64, 4096, 2304], P(('ctx', 'tp'), 'dp')
Inputs may be any that keep to these rules, and one draw needn't show every extreme that they name: `routes`: each row names 8 different experts. Within the rows of one device (aligned blocks of 128 rows) no expert is named more than 12 times, a bound that some block reaches.
All inputs are finite; a program needn't handle non-finite values.
Results may differ from a plain program's by a relative error of at most 0.02.
Values may be sent and summed in bfloat16 or wider, within the bound.
No kernel may reach another device: no remote copies, remote signals or barrier semaphores. Data moves between devices by JAX's collectives and lax.ppermute only.
A program may use at most 192 MiB of HBM per device.

v0:
```python
import jax
import jax.numpy as jnp
from jax import lax
from jax.sharding import PartitionSpec as P


def body(activations, out_grad, routes, gate_probs, saved_pre, expert_weights):
    tok_count = activations.shape[0]
    top_k = routes.shape[1]
    model_width = activations.shape[1]
    ctx_size = lax.axis_size("ctx")
    tp_size = lax.axis_size("tp")
    sources = ctx_size * tp_size
    slots_all = saved_pre.shape[2]
    capacity = slots_all // sources
    hidden = saved_pre.shape[3] // 2
    flat_routes = routes.reshape(-1)
    in_window = flat_routes < sources
    onehot = (flat_routes[:, None] == jnp.arange(sources, dtype=jnp.int32)[None, :]).astype(
        jnp.int32
    )
    position = jnp.sum(jnp.cumsum(onehot, axis=0) * onehot, axis=1) - 1
    slot_index = jnp.where(in_window, flat_routes * capacity + position, sources * capacity)
    route_count = tok_count * top_k
    route_of_slot = jnp.full((sources * capacity,), route_count, jnp.int32)
    route_of_slot = route_of_slot.at[slot_index].set(
        jnp.arange(route_count, dtype=jnp.int32), mode="drop"
    )
    filled = route_of_slot < route_count
    safe_route = jnp.minimum(route_of_slot, route_count - 1)
    token_of_slot = safe_route // top_k
    zero_value = jnp.zeros((), jnp.bfloat16)
    send_rows = jnp.where(filled[:, None], activations[token_of_slot], zero_value)
    send_grads = jnp.where(filled[:, None], out_grad[token_of_slot], zero_value)
    send_probs = jnp.where(filled, gate_probs.reshape(-1)[safe_route], zero_value)
    received = (
        lax.all_to_all(
            send_rows.reshape(sources, capacity, model_width),
            ("ctx", "tp"),
            split_axis=0,
            concat_axis=0,
            tiled=True,
        ),
        lax.all_to_all(
            send_grads.reshape(sources, capacity, model_width),
            ("ctx", "tp"),
            split_axis=0,
            concat_axis=0,
            tiled=True,
        ),
        lax.all_to_all(
            send_probs.reshape(sources, capacity),
            ("ctx", "tp"),
            split_axis=0,
            concat_axis=0,
            tiled=True,
        ),
    )
    recv_rows = received[0].reshape(slots_all, model_width)
    recv_grads = received[1].reshape(slots_all, model_width)
    prob_column = received[2].reshape(slots_all, 1).astype(jnp.float32)
    saved_rows = saved_pre[0, 0]
    pre_gate = saved_rows[:, :hidden].astype(jnp.float32)
    pre_up = saved_rows[:, hidden:].astype(jnp.float32)
    sigmoid_gate = jax.nn.sigmoid(pre_gate)
    activated = pre_gate * sigmoid_gate
    hidden_act = activated * pre_up
    weights = expert_weights[0]
    down_part = weights[:, 2 * hidden :]
    gate_up_part = weights[:, : 2 * hidden]
    down_grad = jnp.dot(
        recv_grads,
        lax.all_gather(down_part, "dp", axis=0, tiled=True),
        preferred_element_type=jnp.float32,
    )
    prob_slot = jnp.sum(hidden_act * down_grad, axis=1).astype(jnp.bfloat16)
    scaled_grad = prob_column * down_grad
    finish_gate_up_grad = jnp.concatenate(
        [
            scaled_grad * pre_up * sigmoid_gate * (1.0 + pre_gate * (1.0 - sigmoid_gate)),
            scaled_grad * activated,
        ],
        axis=1,
    ).astype(jnp.bfloat16)
    finish_scaled_hidden = (prob_column * hidden_act).astype(jnp.bfloat16)
    prob_slot, gate_up_grad, scaled_hidden = (prob_slot, finish_gate_up_grad, finish_scaled_hidden)
    row_grad = lax.dot_general(
        gate_up_grad,
        lax.all_gather(gate_up_part, "dp", axis=0, tiled=True),
        (((1,), (1,)), ((), ())),
        preferred_element_type=jnp.float32,
    ).astype(jnp.bfloat16)
    gate_up_term = lax.dot_general(
        recv_rows, gate_up_grad, (((0,), (0,)), ((), ())), preferred_element_type=jnp.float32
    )
    down_piece = lax.dot_general(
        recv_grads, scaled_hidden, (((0,), (0,)), ((), ())), preferred_element_type=jnp.float32
    )
    weight_grad = lax.psum_scatter(
        jnp.concatenate([gate_up_term, down_piece], axis=1).astype(jnp.bfloat16),
        "dp",
        scatter_dimension=0,
        tiled=True,
    )[None]
    returned = (
        lax.all_to_all(
            row_grad.reshape(sources, capacity, model_width),
            ("ctx", "tp"),
            split_axis=0,
            concat_axis=0,
            tiled=True,
        ),
        lax.all_to_all(
            prob_slot.reshape(sources, capacity),
            ("ctx", "tp"),
            split_axis=0,
            concat_axis=0,
            tiled=True,
        ),
    )
    back_rows = returned[0].reshape(sources * capacity, model_width)
    back_probs = returned[1].reshape(sources * capacity)
    safe_slot = jnp.minimum(slot_index, sources * capacity - 1)
    picked = jnp.where(in_window[:, None], back_rows[safe_slot], zero_value)
    input_grad = jnp.sum(picked.reshape(tok_count, top_k, model_width).astype(jnp.float32), axis=1)
    prob_grad = jnp.where(in_window, back_probs[safe_slot], zero_value).reshape(tok_count, top_k)
    return (input_grad.astype(jnp.bfloat16), prob_grad, weight_grad)


def solution(mesh):
    placed = (
        P(("ctx", "tp", "dp"), None),
        P(("ctx", "tp", "dp"), None),
        P(("ctx", "tp", "dp"), None),
        P(("ctx", "tp", "dp"), None),
        P(("ctx", "tp"), "dp", None, None),
        P(("ctx", "tp"), "dp", None),
    )
    return jax.shard_map(
        body,
        mesh=mesh,
        in_specs=placed,
        out_specs=(
            P(("ctx", "tp", "dp"), None),
            P(("ctx", "tp", "dp"), None),
            P(("ctx", "tp"), "dp", None),
        ),
        check_vma=False,
    )
```

profile of v0, /device:TPU:1, one launch (start us, length us, event | category | flops | bytes accessed | tf_op | source)
XLA Modules:
  0.0 841.0 jit_solution(4453830217344375379)
XLA Ops:
  7.2 0.8 broadcast_multiply_fusion
  8.0 0.8 copy.22
  9.0 0.4 copy-done.5
  9.4 0.8 copy.28
  10.6 18.0 %reduce-window.6 = s32[64,8,128]{2,1,0:T(8,128)S(1)} reduce-window(s32[64,8,128]{2,1,0:T(8,128)S(1)} %fusion.12, s32[]{:T(128)} %constant.18.clone.1), window={size=1x1x128 pad=0_0x0_0x127_0}, to_apply=%region_0.0 | reduce-window | flops 8323072 | bytes 524292 | tf_op jit(solution)/shard_map/reduce-window
  28.6 0.1 slice.34
  28.8 0.1 copy.26
  29.1 0.1 broadcast_add_fusion
  29.3 0.6 compare_select_fusion
  29.9 4.3 scatter_custom_fusion
  34.2 5.0 gather_fusion
  39.2 0.7 all_to_all.25
  40.0 12.3 %all-to-all-start = ((bf16[64,1,12]{2,1,0:T(2,128)(2,1)}), bf16[64,1,12]{2,1,0:T(2,128)(2,1)S(1)}, u32[]{:S(2)}, u32[]{:S(2)}) async-start(bf16[64,1,12]{2,1,0:T(2,128)(2,1)} %all_to_all.25), calls=%async_computation | async-start | bytes 65536 | tf_op jit(solution)/shard_map/all_to_all | solution.py:51
  52.4 5.7 gather_fusion.4
  58.1 9.9 %gather.31 = bf16[64,12,4096]{2,1,0:T(8,128)(2,1)} reshape(bf16[768,4096]{1,0:T(8,128)(2,1)} %gather_fusion.4) | data formatting | bytes 12582912 | tf_op jit(solution)/shard_map/gather | solution.py:33
  68.0 5.7 gather_fusion.1
  73.7 9.7 %gather.25 = bf16[64,12,4096]{2,1,0:T(8,128)(2,1)} reshape(bf16[768,4096]{1,0:T(8,128)(2,1)} %gather_fusion.1) | data formatting | bytes 12582912 | tf_op jit(solution)/shard_map/gather | solution.py:34
  83.5 11.6 %broadcast_select_fusion = (bf16[64,12,4096]{2,1,0:T(8,128)(2,1)}, bf16[64,12,4096]{2,1,0:T(8,128)(2,1)}) fusion(bf16[64,12,4096]{2,1,0:T(8,128)(2,1)} %gather.31, pred[64,12]{1,0:T(8,128)(4,1)S(1)} %broadcast_in_dim.63, bf16[64,12,4096]{2,1,0:T(8,128)(2,1)} %gather.25), kind=kLoop, calls=%fused_computation.10 | loop fusion | flops 6291456 | bytes 25166592 | tf_op jit(solution)/shard_map/jit(_where)/select_n | solution.py:33
  95.0 10.5 %all-to-all-start.4 = ((bf16[64,12,4096]{2,1,0:T(8,128)(2,1)}), bf16[64,12,4096]{2,1,0:T(8,128)(2,1)}, u32[]{:S(2)}, u32[]{:S(2)}) async-start(bf16[64,12,4096]{2,1,0:T(8,128)(2,1)} %get-tuple-element.19), calls=%async_computation.4 | async-start | bytes 16777216 | tf_op jit(solution)/shard_map/all_to_all | solution.py:37
  105.6 3.7 slice.36
  109.3 95.8 %all-to-all-done.4 = bf16[64,12,4096]{2,1,0:T(8,128)(2,1)} async-done(((bf16[64,12,4096]{2,1,0:T(8,128)(2,1)}), bf16[64,12,4096]{2,1,0:T(8,128)(2,1)}, u32[]{:S(2)}, u32[]{:S(2)}) %all-to-all-start.4) | async-done | bytes 6291488 | tf_op jit(solution)/shard_map/all_to_all | solution.py:37
  205.1 19.6 %all-to-all-start.1 = ((bf16[64,12,4096]{2,1,0:T(8,128)(2,1)}), bf16[64,12,4096]{2,1,0:T(8,128)(2,1)}, u32[]{:S(2)}, u32[]{:S(2)}) async-start(bf16[64,12,4096]{2,1,0:T(8,128)(2,1)} %get-tuple-element.20), calls=%async_computation.1 | async-start | bytes 16777216 | tf_op jit(solution)/shard_map/all_to_all | solution.py:44
  224.7 5.9 slice.39
  230.7 0.5 reduce-scatter.2.cloned.1.call-start
  231.2 1.1 copy-done.3
  232.3 2.5 copy.30
  235.0 10.0 %reshape.174 = bf16[768,4096]{1,0:T(8,128)(2,1)} reshape(bf16[64,12,4096]{2,1,0:T(8,128)(2,1)} %all-to-all-done.4) | data formatting | bytes 12582912 | tf_op jit(solution)/shard_map/reshape | solution.py:59
  245.0 79.3 %all-to-all-done.1 = bf16[64,12,4096]{2,1,0:T(8,128)(2,1)} async-done(((bf16[64,12,4096]{2,1,0:T(8,128)(2,1)}), bf16[64,12,4096]{2,1,0:T(8,128)(2,1)}, u32[]{:S(2)}, u32[]{:S(2)}) %all-to-all-start.1) | async-done | bytes 6291488 | tf_op jit(solution)/shard_map/all_to_all | solution.py:44
  324.3 9.8 %reshape.170 = bf16[768,4096]{1,0:T(8,128)(2,1)} reshape(bf16[64,12,4096]{2,1,0:T(8,128)(2,1)} %all-to-all-done.1) | data formatting | bytes 12582912 | tf_op jit(solution)/shard_map/reshape | solution.py:60
  334.1 10.0 %convolution_convert_fusion.1 = bf16[4096,768]{0,1:T(8,128)(2,1)} fusion(bf16[768,4096]{1,0:T(8,128)(2,1)} %reshape.170, f32[768]{0:T(1024)S(1)} %reshape.175, bf16[768,1536]{0,1:T(8,128)(2,1)S(1)} %bitcast.33), kind=kOutput, calls=%fused_computation.12 | convolution fusion | flops 4840292352 | bytes 14945280 | tf_op jit(solution)/shard_map/dot_general | solution.py:96
  344.1 10.4 %all-gather.3.cloned.1.call-done = bf16[4096,768]{1,0:T(8,128)(2,1)} async-done(((bf16[2048,768]{1,0:T(8,128)(2,1)}), bf16[4096,768]{1,0:T(8,128)(2,1)}) %all-gather.3.cloned.1.call-update) | async-done | bytes 6291472 | tf_op jit(solution)/shard_map/all_gather | solution.py:73
  354.5 11.0 %fusion.3 = (bf16[768,768]{0,1:T(8,128)(2,1)S(1)}, bf16[768,768]{0,1:T(8,128)(2,1)}, bf16[768]{0:T(1024)(128)(2,1)S(1)}) fusion(f32[768]{0:T(1024)S(1)} %reshape.175, bf16[768,1536]{0,1:T(8,128)(2,1)S(1)} %bitcast.34, bf16[768,4096]{1,0:T(8,128)(2,1)} %reshape.170, bf16[4096,768]{1,0:T(8,128)(2,1)} %all-gather.3.cloned.1.call-done), kind=kOutput, calls=%fused_computation.21 | convolution fusion | flops 4843043840 | bytes 17306112 | tf_op jit(solution)/shard_map/dot_general | solution.py:71
  365.5 13.5 %convolution_convert_fusion = bf16[4096,1536]{0,1:T(8,128)(2,1)S(1)} fusion(bf16[768,4096]{1,0:T(8,128)(2,1)} %reshape.174, bf16[768,768]{0,1:T(8,128)(2,1)} %get-tuple-element.15, bf16[768,768]{0,1:T(8,128)(2,1)S(1)} %get-tuple-element.14), kind=kOutput, calls=%fused_computation.7 | convolution fusion | flops 9674686464 | bytes 21233664 | tf_op jit(solution)/shard_map/dot_general | solution.py:93
  379.0 17.0 %pad_maximum_fusion = bf16[4096,2304]{0,1:T(8,128)(2,1)} fusion(bf16[4096,768]{0,1:T(8,128)(2,1)} %convolution_convert_fusion.1, bf16[4096,1536]{0,1:T(8,128)(2,1)S(1)} %convolution_convert_fusion), kind=kLoop, calls=%fused_computation.6 | loop fusion | flops 37748736 | bytes 37748736 | tf_op jit(solution)/shard_map/concatenate | solution.py:100
  396.0 0.7 convert_element_type.56
  396.7 11.3 %all-to-all-start.3 = ((bf16[64,1,12]{2,1,0:T(2,128)(2,1)}), bf16[64,1,12]{2,1,0:T(2,128)(2,1)S(1)}, u32[]{:S(2)}, u32[]{:S(2)}) async-start(bf16[64,1,12]{2,1,0:T(2,128)(2,1)} %convert_element_type.56), calls=%async_computation.3 | async-start | bytes 65536 | tf_op jit(solution)/shard_map/all_to_all | solution.py:113
  408.0 105.9 %all-gather.5.cloned.1.call-done = bf16[4096,1536]{1,0:T(8,128)(2,1)} async-done(((bf16[2048,1536]{1,0:T(8,128)(2,1)}), bf16[4096,1536]{1,0:T(8,128)(2,1)}) %all-gather.5.cloned.1.call-update) | async-done | bytes 12582928 | tf_op jit(solution)/shard_map/all_gather | solution.py:89
  513.9 14.7 %convolution_convert_fusion.2 = bf16[768,4096]{1,0:T(8,128)(2,1)} fusion(bf16[4096,1536]{1,0:T(8,128)(2,1)} %all-gather.5.cloned.1.call-done, bf16[768,768]{0,1:T(8,128)(2,1)S(1)} %copy-done.12, bf16[768,768]{0,1:T(8,128)(2,1)S(1)} %copy-done.11), kind=kOutput, calls=%fused_computation.13 | convolution fusion | flops 9671540736 | bytes 21233664 | tf_op jit(solution)/shard_map/dot_general | solution.py:87
  528.6 9.8 %reshape.171 = bf16[64,12,4096]{2,1,0:T(8,128)(2,1)} reshape(bf16[768,4096]{1,0:T(8,128)(2,1)} %convolution_convert_fusion.2) | data formatting | bytes 12582912 | tf_op jit(solution)/shard_map/reshape | solution.py:107
  538.5 11.1 %all-to-all-start.2 = ((bf16[64,12,4096]{2,1,0:T(8,128)(2,1)}), bf16[64,12,4096]{2,1,0:T(8,128)(2,1)}, u32[]{:S(2)}, u32[]{:S(2)}) async-start(bf16[64,12,4096]{2,1,0:T(8,128)(2,1)} %reshape.171), calls=%async_computation.2 | async-start | bytes 16777216 | tf_op jit(solution)/shard_map/all_to_all | solution.py:106
  549.8 6.8 gather_fusion.3
  556.7 0.7 copy.32
  557.4 92.3 %all-to-all-done.2 = bf16[64,12,4096]{2,1,0:T(8,128)(2,1)} async-done(((bf16[64,12,4096]{2,1,0:T(8,128)(2,1)}), bf16[64,12,4096]{2,1,0:T(8,128)(2,1)}, u32[]{:S(2)}, u32[]{:S(2)}) %all-to-all-start.2) | async-done | bytes 6291488 | tf_op jit(solution)/shard_map/all_to_all | solution.py:106
  649.7 10.0 %reshape.172 = bf16[768,4096]{1,0:T(8,128)(2,1)} reshape(bf16[64,12,4096]{2,1,0:T(8,128)(2,1)} %all-to-all-done.2) | data formatting | bytes 12582912 | tf_op jit(solution)/shard_map/reshape | solution.py:121
  659.7 18.7 %gather_fusion.2 = bf16[1024,4096]{1,0:T(8,128)(2,1)} fusion(bf16[768,4096]{1,0:T(8,128)(2,1)} %reshape.172, s32[1024]{0:T(1024)S(1)} %broadcast_clamp_fusion), kind=kCustom, calls=%fused_computation.2 | custom fusion | bytes 16781312 | tf_op jit(solution)/shard_map/gather | solution.py:124
  678.3 8.5 %fusion = bf16[128,4096]{1,0:T(8,128)(2,1)} fusion(bf16[1024,4096]{1,0:T(8,128)(2,1)} %gather_fusion.2, pred[128,8]{1,0:T(8,128)(4,1)S(1)} %copy-done.8), kind=kLoop, calls=%fused_computation.9 | loop fusion | flops 7864320 | bytes 9438208 | tf_op jit(solution)/shard_map/reduce_sum | solution.py:125
  686.8 134.7 %reduce-scatter.2.cloned.1.call-done = bf16[2048,2304]{0,1:T(8,128)(2,1)} async-done(((bf16[4096,2304]{0,1:T(8,128)(2,1)}), bf16[2048,2304]{0,1:T(8,128)(2,1)}) %reduce-scatter.2.cloned.1.call-update) | async-done | bytes 9437200 | tf_op jit(solution)/shard_map/reduce_scatter | solution.py:99
  821.5 12.7 %copy.33 = bf16[1,2048,2304]{2,1,0:T(8,128)(2,1)} copy(bf16[1,2048,2304]{1,2,0:T(8,128)(2,1)} %bitcast.32) | data formatting | bytes 18874368
  (56 shorter events, 1.6 us)
Async XLA Ops:
  7.2 45.2 %copy-start = (bf16[128,4096]{1,0:T(8,128)(2,1)S(1)}, bf16[128,4096]{1,0:T(8,128)(2,1)}, u32[]{:S(2)}) copy-start(bf16[128,4096]{1,0:T(8,128)(2,1)} %param.6) | copy-start | bytes 3145732
  8.7 0.6 copy-start.5
  9.4 1.2 copy-start.7
  40.0 55.0 %all-to-all-start = ((bf16[64,1,12]{2,1,0:T(2,128)(2,1)}), bf16[64,1,12]{2,1,0:T(2,128)(2,1)S(1)}, u32[]{:S(2)}, u32[]{:S(2)}) async-start(bf16[64,1,12]{2,1,0:T(2,128)(2,1)} %all_to_all.25), calls=%async_computation | async-start | bytes 65536 | tf_op jit(solution)/shard_map/all_to_all | solution.py:51
  58.1 9.9 %copy-start.2 = (bf16[128,4096]{1,0:T(8,128)(2,1)S(1)}, bf16[128,4096]{1,0:T(8,128)(2,1)}, u32[]{:S(2)}) copy-start(bf16[128,4096]{1,0:T(8,128)(2,1)} %param.7) | copy-start | bytes 3145732
  95.0 110.1 %all-to-all-start.4 = ((bf16[64,12,4096]{2,1,0:T(8,128)(2,1)}), bf16[64,12,4096]{2,1,0:T(8,128)(2,1)}, u32[]{:S(2)}, u32[]{:S(2)}) async-start(bf16[64,12,4096]{2,1,0:T(8,128)(2,1)} %get-tuple-element.19), calls=%async_computation.4 | async-start | bytes 16777216 | tf_op jit(solution)/shard_map/all_to_all | solution.py:37
  105.5 249.0 %all-gather.3.cloned.1.call-start = ((), (), s32[]{:S(2)}) async-start(), calls=%async_computation.6 | async-start | bytes 9437184 | tf_op jit(solution)/shard_map/all_gather | solution.py:73
  205.1 119.2 %all-to-all-start.1 = ((bf16[64,12,4096]{2,1,0:T(8,128)(2,1)}), bf16[64,12,4096]{2,1,0:T(8,128)(2,1)}, u32[]{:S(2)}, u32[]{:S(2)}) async-start(bf16[64,12,4096]{2,1,0:T(8,128)(2,1)} %get-tuple-element.20), calls=%async_computation.1 | async-start | bytes 16777216 | tf_op jit(solution)/shard_map/all_to_all | solution.py:44
  224.7 289.2 %all-gather.5.cloned.1.call-start = ((), (), s32[]{:S(2)}) async-start(), calls=%async_computation.7 | async-start | bytes 18874368 | tf_op jit(solution)/shard_map/all_gather | solution.py:89
  230.6 1.7 copy-start.3
  230.7 590.8 %reduce-scatter.2.cloned.1.call-start = ((), (), s32[]{:S(2)}) async-start(), calls=%async_computation.8 | async-start | bytes 28311552 | tf_op jit(solution)/shard_map/reduce_scatter | solution.py:99
  245.0 89.2 %copy-start.4 = (bf16[1,1,768,1536]{2,3,1,0:T(8,128)(2,1)S(1)}, bf16[1,1,768,1536]{2,3,1,0:T(8,128)(2,1)}, u32[]{:S(2)}) copy-start(bf16[1,1,768,1536]{2,3,1,0:T(8,128)(2,1)} %copy.30) | copy-start | bytes 7077892
  365.5 13.5 %copy-start.10 = (bf16[768,768]{0,1:T(8,128)(2,1)}, bf16[768,768]{0,1:T(8,128)(2,1)S(1)}, u32[]{:S(2)}) copy-start(bf16[768,768]{0,1:T(8,128)(2,1)S(1)} %get-tuple-element.14) | copy-start | bytes 3538948
  395.9 117.9 %copy-start.11 = (bf16[768,768]{0,1:T(8,128)(2,1)S(1)}, bf16[768,768]{0,1:T(8,128)(2,1)}, u32[]{:S(2)}) copy-start(bf16[768,768]{0,1:T(8,128)(2,1)} %copy-done.10) | copy-start | bytes 3538948
  395.9 117.9 %copy-start.12 = (bf16[768,768]{0,1:T(8,128)(2,1)S(1)}, bf16[768,768]{0,1:T(8,128)(2,1)}, u32[]{:S(2)}) copy-start(bf16[768,768]{0,1:T(8,128)(2,1)} %get-tuple-element.15) | copy-start | bytes 3538948
  396.7 141.8 %all-to-all-start.3 = ((bf16[64,1,12]{2,1,0:T(2,128)(2,1)}), bf16[64,1,12]{2,1,0:T(2,128)(2,1)S(1)}, u32[]{:S(2)}, u32[]{:S(2)}) async-start(bf16[64,1,12]{2,1,0:T(2,128)(2,1)} %convert_element_type.56), calls=%async_computation.3 | async-start | bytes 65536 | tf_op jit(solution)/shard_map/all_to_all | solution.py:113
  538.5 11.1 %copy-start.9 = (s32[1024,1]{0,1:T(1,128)S(1)}, s32[1024,1]{0,1:T(1,128)}, u32[]{:S(2)}) copy-start(s32[1024,1]{0,1:T(1,128)} %get-tuple-element.17) | copy-start | bytes 12292
  538.5 18.2 %copy-start.6 = (s32[128,8]{1,0:T(8,128)S(1)}, s32[128,8]{1,0:T(8,128)}, u32[]{:S(2)}) copy-start(s32[128,8]{1,0:T(8,128)} %copy-done.5) | copy-start | bytes 12292
  538.5 111.2 %all-to-all-start.2 = ((bf16[64,12,4096]{2,1,0:T(8,128)(2,1)}), bf16[64,12,4096]{2,1,0:T(8,128)(2,1)}, u32[]{:S(2)}, u32[]{:S(2)}) async-start(bf16[64,12,4096]{2,1,0:T(8,128)(2,1)} %reshape.171), calls=%async_computation.2 | async-start | bytes 16777216 | tf_op jit(solution)/shard_map/all_to_all | solution.py:106
  659.6 18.7 %copy-start.8 = (pred[128,8]{1,0:T(8,128)(4,1)S(1)}, pred[128,8]{1,0:T(8,128)(4,1)}, u32[]{:S(2)}) copy-start(pred[128,8]{1,0:T(8,128)(4,1)} %copy-done.7) | copy-start | bytes 3076
  821.5 12.7 %copy-start.1 = (bf16[128,4096]{1,0:T(8,128)(2,1)S(1)}, bf16[128,4096]{1,0:T(8,128)(2,1)}, u32[]{:S(2)}) copy-start(bf16[128,4096]{1,0:T(8,128)(2,1)} %param.6) | copy-start | bytes 3145732
Sparse Core Ops, SparseCore 0:
  109.4 245.0 all-gather.2
  356.7 157.0 all-gather.4
  516.3 305.1 reduce-scatter.1
where the time goes:
time: 850 us; the launch traced here: 841 us
  waiting for transfers between devices  518 us (61%)
  local copies, waits for them, and re-layouts  137 us (16%)
  starting transfers between devices  65.3 us (8%)
  other arithmetic  56.9 us (7%)
  matrix products  49.2 us (6%)
  between operations  14.2 us (2%)
    reduce_scatter x1, waiting for transfers between devices, body(): lax.psum_scatter(jnp.concatenate([gate_up_term, down_piece], axis=1).asty...  135 us
    all_gather x1, waiting for transfers between devices, body(): lax.all_gather(gate_up_part, 'dp', axis=0, tiled=True)  106 us
    all_to_all x1, waiting for transfers between devices, body(): lax.all_to_all(send_rows.reshape(sources, capacity, model_width), ('ctx',...  95.8 us
    all_to_all x1, waiting for transfers between devices, body(): lax.all_to_all(row_grad.reshape(sources, capacity, model_width), ('ctx',...  92.3 us
    all_to_all x1, waiting for transfers between devices, body(): lax.all_to_all(send_grads.reshape(sources, capacity, model_width), ('ctx'...  79.3 us
    all_to_all x1, starting transfers between devices, body(): lax.all_to_all(send_grads.reshape(sources, capacity, model_width), ('ctx'...  19.6 us
    unnamed x31, local copies, waits for them, and re-layouts  19 us
    gather x1, local copies, waits for them, and re-layouts, body(): picked = jnp.where(in_window[:, None], back_rows[safe_slot], zero_value)  18.7 us
  transfers between devices with their start and end apart: 8, of which 6 were waited for; matrix products, arithmetic and copies ran while one was open for 23% of the time, Pallas kernels for 0%

commit v1 on v0

--- a/solution.py
+++ b/solution.py
@@ -86,7 +86,9 @@
     prob_slot, gate_up_grad, scaled_hidden = (prob_slot, finish_gate_up_grad, finish_scaled_hidden)
     row_grad = lax.dot_general(
         gate_up_grad,
-        lax.all_gather(gate_up_part, "dp", axis=0, tiled=True),
+        jnp.concatenate(
+            lax.all_to_all(jnp.stack([gate_up_part] * lax.axis_size("dp")), "dp", 0, 0), axis=0
+        ),
         (((1,), (1,)), ((), ())),
         preferred_element_type=jnp.float32,
     ).astype(jnp.bfloat16)

time: 850 us -> 923 us (1.086)
  blocking collectives: 0 us -> 107 us
  waiting for transfers between devices: 518 us -> 486 us
  starting transfers between devices: 65.3 us -> 52.1 us
    all_to_all x1, waiting for transfers between devices: 95.8 us -> 272 us  [body(): lax.all_to_all(jnp.stack([gate_up_part] * lax.axis_size('dp')), 'dp', 0, 0)]
    reduce_scatter x1, waiting for transfers between devices: 135 us -> 0.01 us  [body(): lax.psum_scatter(jnp.concatenate([gate_up_term, down_piece], axis=1).asty...]
    all_to_all x0 -> x1, blocking collectives: none -> 107 us  [body(): lax.all_to_all(send_rows.reshape(sources, capacity, model_width), ('ctx',...]
    all_gather x1 -> x0, waiting for transfers between devices: 106 us -> none  [body(): lax.all_gather(gate_up_part, 'dp', axis=0, tiled=True)]
    all_gather x1, waiting for transfers between devices: 10.4 us -> 39.6 us  [body(): lax.all_gather(down_part, 'dp', axis=0, tiled=True)]
    all_to_all x1, starting transfers between devices: 19.6 us -> 7.82 us  [body(): lax.all_to_all(send_grads.reshape(sources, capacity, model_width), ('ctx'...]
    another operation x3 -> x4, other arithmetic: 18.2 us -> 23.7 us
  transfers between devices with their start and end apart: 8 -> 7, of which waited for: 6 -> 4; matrix products, arithmetic and copies ran while one was open for 23% -> 17% of each run, Pallas kernels for 0% -> 0%
where the time goes in v1:
time: 923 us; the launch traced here: 905 us
  waiting for transfers between devices  486 us (53%)
  local copies, waits for them, and re-layouts  134 us (15%)
  blocking collectives  107 us (12%)
  other arithmetic  62.5 us (7%)
  starting transfers between devices  52.1 us (6%)
  matrix products  48.4 us (5%)
  between operations  14.6 us (2%)
    all_to_all x1, waiting for transfers between devices, body(): lax.all_to_all(jnp.stack([gate_up_part] * lax.axis_size('dp')), 'dp', 0, 0)  272 us
    all_to_all x1, blocking collectives, body(): lax.all_to_all(send_rows.reshape(sources, capacity, model_width), ('ctx',...  107 us
    all_to_all x1, waiting for transfers between devices, body(): lax.all_to_all(row_grad.reshape(sources, capacity, model_width), ('ctx',...  92.5 us
    all_to_all x1, waiting for transfers between devices, body(): lax.all_to_all(send_grads.reshape(sources, capacity, model_width), ('ctx'...  82.3 us
    all_gather x1, waiting for transfers between devices, body(): lax.all_gather(down_part, 'dp', axis=0, tiled=True)  39.6 us
    gather x1, local copies, waits for them, and re-layouts, body(): picked = jnp.where(in_window[:, None], back_rows[safe_slot], zero_value)  18.7 us
  transfers between devices with their start and end apart: 7, of which 4 were waited for; matrix products, arithmetic and copies ran while one was open for 17% of the time, Pallas kernels for 0%

profile of v1, /device:TPU:1, one launch (start us, length us, event | category | flops | bytes accessed | tf_op | source)
XLA Modules:
  0.0 904.9 jit_solution(4698494350534599696)
XLA Ops:
  7.2 0.8 broadcast_multiply_fusion
  8.0 0.8 copy.22
  9.0 0.4 copy-done.5
  9.4 0.8 copy.28
  10.6 18.0 %reduce-window.6 = s32[64,8,128]{2,1,0:T(8,128)S(1)} reduce-window(s32[64,8,128]{2,1,0:T(8,128)S(1)} %fusion.12, s32[]{:T(128)} %constant.18.clone.1), window={size=1x1x128 pad=0_0x0_0x127_0}, to_apply=%region_0.0 | reduce-window | flops 8323072 | bytes 524292 | tf_op jit(solution)/shard_map/reduce-window
  28.6 0.1 slice.34
  28.8 0.1 copy.26
  29.1 0.1 broadcast_add_fusion
  29.3 0.6 compare_select_fusion
  29.9 4.3 scatter_custom_fusion
  34.2 5.0 gather_fusion
  39.2 0.7 all_to_all.29
  40.0 12.3 %all-to-all-start = ((bf16[64,1,12]{2,1,0:T(2,128)(2,1)}), bf16[64,1,12]{2,1,0:T(2,128)(2,1)S(1)}, u32[]{:S(2)}, u32[]{:S(2)}) async-start(bf16[64,1,12]{2,1,0:T(2,128)(2,1)} %all_to_all.29), calls=%async_computation | async-start | bytes 65536 | tf_op jit(solution)/shard_map/all_to_all | solution.py:51
  52.4 5.7 gather_fusion.4
  58.1 9.9 %gather.31 = bf16[64,12,4096]{2,1,0:T(8,128)(2,1)} reshape(bf16[768,4096]{1,0:T(8,128)(2,1)} %gather_fusion.4) | data formatting | bytes 12582912 | tf_op jit(solution)/shard_map/gather | solution.py:33
  68.0 5.7 gather_fusion.1
  73.7 9.8 %gather.25 = bf16[64,12,4096]{2,1,0:T(8,128)(2,1)} reshape(bf16[768,4096]{1,0:T(8,128)(2,1)} %gather_fusion.1) | data formatting | bytes 12582912 | tf_op jit(solution)/shard_map/gather | solution.py:34
  83.5 11.6 %broadcast_select_fusion = (bf16[64,12,4096]{2,1,0:T(8,128)(2,1)}, bf16[64,12,4096]{2,1,0:T(8,128)(2,1)}) fusion(bf16[64,12,4096]{2,1,0:T(8,128)(2,1)} %gather.31, pred[64,12]{1,0:T(8,128)(4,1)S(1)} %broadcast_in_dim.63, bf16[64,12,4096]{2,1,0:T(8,128)(2,1)} %gather.25), kind=kLoop, calls=%fused_computation.11 | loop fusion | flops 6291456 | bytes 25166592 | tf_op jit(solution)/shard_map/jit(_where)/select_n | solution.py:33
  95.1 107.4 %all_to_all.36 = bf16[64,12,4096]{2,1,0:T(8,128)(2,1)} all-to-all(bf16[64,12,4096]{2,1,0:T(8,128)(2,1)} %get-tuple-element.19), channel_id=1, replica_groups=mesh['ctx'=8,'tp'=8,'dp'=2] {'ctx','tp'}, dimensions={0} | all-to-all | bytes 12582912 | tf_op jit(solution)/shard_map/all_to_all | solution.py:37
  202.4 7.8 all-to-all-start.1
  210.3 3.9 slice.36
  214.2 0.5 reduce-scatter.2.cloned.1.call-start
  214.7 2.5 copy.30
  217.4 10.1 %reshape.178 = bf16[768,4096]{1,0:T(8,128)(2,1)} reshape(bf16[64,12,4096]{2,1,0:T(8,128)(2,1)} %all_to_all.36) | data formatting | bytes 12582912 | tf_op jit(solution)/shard_map/reshape | solution.py:59
  227.5 82.3 %all-to-all-done.1 = bf16[64,12,4096]{2,1,0:T(8,128)(2,1)} async-done(((bf16[64,12,4096]{2,1,0:T(8,128)(2,1)}), bf16[64,12,4096]{2,1,0:T(8,128)(2,1)}, u32[]{:S(2)}, u32[]{:S(2)}) %all-to-all-start.1) | async-done | bytes 6291488 | tf_op jit(solution)/shard_map/all_to_all | solution.py:44
  309.8 9.9 %reshape.173 = bf16[768,4096]{1,0:T(8,128)(2,1)} reshape(bf16[64,12,4096]{2,1,0:T(8,128)(2,1)} %all-to-all-done.1) | data formatting | bytes 12582912 | tf_op jit(solution)/shard_map/reshape | solution.py:60
  319.8 9.9 %convolution_convert_fusion.1 = bf16[4096,768]{0,1:T(8,128)(2,1)} fusion(bf16[768,4096]{1,0:T(8,128)(2,1)} %reshape.173, f32[768]{0:T(1024)S(1)} %reshape.179, bf16[768,1536]{0,1:T(8,128)(2,1)S(1)} %bitcast.36), kind=kOutput, calls=%fused_computation.13 | convolution fusion | flops 4840292352 | bytes 14945280 | tf_op jit(solution)/shard_map/dot_general | solution.py:98
  329.7 39.6 %all-gather.2.cloned.1.call-done = bf16[4096,768]{1,0:T(8,128)(2,1)} async-done(((bf16[2048,768]{1,0:T(8,128)(2,1)}), bf16[4096,768]{1,0:T(8,128)(2,1)}) %all-gather.2.cloned.1.call-update) | async-done | bytes 6291472 | tf_op jit(solution)/shard_map/all_gather | solution.py:73
  369.3 11.0 %fusion.3 = (bf16[768,768]{0,1:T(8,128)(2,1)S(1)}, bf16[768,768]{0,1:T(8,128)(2,1)}, bf16[768]{0:T(1024)(128)(2,1)S(1)}) fusion(f32[768]{0:T(1024)S(1)} %reshape.179, bf16[768,1536]{0,1:T(8,128)(2,1)S(1)} %bitcast.37, bf16[768,4096]{1,0:T(8,128)(2,1)} %reshape.173, bf16[4096,768]{1,0:T(8,128)(2,1)} %all-gather.2.cloned.1.call-done), kind=kOutput, calls=%fused_computation.23 | convolution fusion | flops 4843043840 | bytes 17306112 | tf_op jit(solution)/shard_map/dot_general | solution.py:71
  380.3 12.9 %convolution_convert_fusion = bf16[4096,1536]{0,1:T(8,128)(2,1)S(1)} fusion(bf16[768,4096]{1,0:T(8,128)(2,1)} %reshape.178, bf16[768,768]{0,1:T(8,128)(2,1)} %get-tuple-element.15, bf16[768,768]{0,1:T(8,128)(2,1)S(1)} %get-tuple-element.14), kind=kOutput, calls=%fused_computation.7 | convolution fusion | flops 9674686464 | bytes 21233664 | tf_op jit(solution)/shard_map/dot_general | solution.py:95
  393.2 17.0 %pad_maximum_fusion = bf16[4096,2304]{0,1:T(8,128)(2,1)} fusion(bf16[4096,768]{0,1:T(8,128)(2,1)} %convolution_convert_fusion.1, bf16[4096,1536]{0,1:T(8,128)(2,1)S(1)} %convolution_convert_fusion), kind=kLoop, calls=%fused_computation.6 | loop fusion | flops 37748736 | bytes 37748736 | tf_op jit(solution)/shard_map/concatenate | solution.py:102
  410.2 3.2 slice_bitcast_fusion
  413.4 5.5 pad_maximum_fusion.1
  418.9 8.8 all-to-all-start.2
  427.7 0.7 convert_element_type.56
  428.5 271.8 %all-to-all-done.2 = bf16[2,2048,1536]{2,1,0:T(8,128)(2,1)} async-done(((bf16[2,2048,1536]{2,1,0:T(8,128)(2,1)}), bf16[2,2048,1536]{2,1,0:T(8,128)(2,1)}, u32[]{:S(2)}, u32[]{:S(2)}) %all-to-all-start.2) | async-done | bytes 12582944 | tf_op jit(solution)/shard_map/all_to_all | solution.py:90
  700.2 11.6 %all-to-all-start.4 = ((bf16[64,1,12]{2,1,0:T(2,128)(2,1)}), bf16[64,1,12]{2,1,0:T(2,128)(2,1)S(1)}, u32[]{:S(2)}, u32[]{:S(2)}) async-start(bf16[64,1,12]{2,1,0:T(2,128)(2,1)} %convert_element_type.56), calls=%async_computation.4 | async-start | bytes 65536 | tf_op jit(solution)/shard_map/all_to_all | solution.py:115
  711.9 14.6 %convolution_convert_fusion.2 = bf16[768,4096]{1,0:T(8,128)(2,1)} fusion(bf16[4096,1536]{1,0:T(8,128)(2,1)} %bitcast.7, bf16[768,768]{0,1:T(8,128)(2,1)S(1)} %copy-done.12, bf16[768,768]{0,1:T(8,128)(2,1)S(1)} %copy-done.11), kind=kOutput, calls=%fused_computation.14 | convolution fusion | flops 9671540736 | bytes 21233664 | tf_op jit(solution)/shard_map/dot_general | solution.py:87
  726.5 10.2 %reshape.175 = bf16[64,12,4096]{2,1,0:T(8,128)(2,1)} reshape(bf16[768,4096]{1,0:T(8,128)(2,1)} %convolution_convert_fusion.2) | data formatting | bytes 12582912 | tf_op jit(solution)/shard_map/reshape | solution.py:109
  736.7 11.1 %all-to-all-start.3 = ((bf16[64,12,4096]{2,1,0:T(8,128)(2,1)}), bf16[64,12,4096]{2,1,0:T(8,128)(2,1)}, u32[]{:S(2)}, u32[]{:S(2)}) async-start(bf16[64,12,4096]{2,1,0:T(8,128)(2,1)} %reshape.175), calls=%async_computation.3 | async-start | bytes 16777216 | tf_op jit(solution)/shard_map/all_to_all | solution.py:108
  747.9 0.1 reshape.177
  748.0 6.8 gather_fusion.3
  754.9 0.7 copy.32
  755.6 92.5 %all-to-all-done.3 = bf16[64,12,4096]{2,1,0:T(8,128)(2,1)} async-done(((bf16[64,12,4096]{2,1,0:T(8,128)(2,1)}), bf16[64,12,4096]{2,1,0:T(8,128)(2,1)}, u32[]{:S(2)}, u32[]{:S(2)}) %all-to-all-start.3) | async-done | bytes 6291488 | tf_op jit(solution)/shard_map/all_to_all | solution.py:108
  848.1 9.9 %reshape.176 = bf16[768,4096]{1,0:T(8,128)(2,1)} reshape(bf16[64,12,4096]{2,1,0:T(8,128)(2,1)} %all-to-all-done.3) | data formatting | bytes 12582912 | tf_op jit(solution)/shard_map/reshape | solution.py:123
  858.0 18.7 %gather_fusion.2 = bf16[1024,4096]{1,0:T(8,128)(2,1)} fusion(bf16[768,4096]{1,0:T(8,128)(2,1)} %reshape.176, s32[1024]{0:T(1024)S(1)} %broadcast_clamp_fusion), kind=kCustom, calls=%fused_computation.2 | custom fusion | bytes 16781312 | tf_op jit(solution)/shard_map/gather | solution.py:126
  876.6 8.5 fusion
  885.2 12.7 %copy.33 = bf16[1,2048,2304]{2,1,0:T(8,128)(2,1)} copy(bf16[1,2048,2304]{1,2,0:T(8,128)(2,1)} %bitcast.35) | data formatting | bytes 18874368
  (55 shorter events, 1.5 us)
Async XLA Ops:
  7.2 45.2 %copy-start = (bf16[128,4096]{1,0:T(8,128)(2,1)S(1)}, bf16[128,4096]{1,0:T(8,128)(2,1)}, u32[]{:S(2)}) copy-start(bf16[128,4096]{1,0:T(8,128)(2,1)} %param.6) | copy-start | bytes 3145732
  8.7 0.6 copy-start.5
  9.4 1.2 copy-start.7
  40.0 55.1 %all-to-all-start = ((bf16[64,1,12]{2,1,0:T(2,128)(2,1)}), bf16[64,1,12]{2,1,0:T(2,128)(2,1)S(1)}, u32[]{:S(2)}, u32[]{:S(2)}) async-start(bf16[64,1,12]{2,1,0:T(2,128)(2,1)} %all_to_all.29), calls=%async_computation | async-start | bytes 65536 | tf_op jit(solution)/shard_map/all_to_all | solution.py:51
  58.1 9.9 %copy-start.2 = (bf16[128,4096]{1,0:T(8,128)(2,1)S(1)}, bf16[128,4096]{1,0:T(8,128)(2,1)}, u32[]{:S(2)}) copy-start(bf16[128,4096]{1,0:T(8,128)(2,1)} %param.7) | copy-start | bytes 3145732
  202.4 107.4 %all-to-all-start.1 = ((bf16[64,12,4096]{2,1,0:T(8,128)(2,1)}), bf16[64,12,4096]{2,1,0:T(8,128)(2,1)}, u32[]{:S(2)}, u32[]{:S(2)}) async-start(bf16[64,12,4096]{2,1,0:T(8,128)(2,1)} %get-tuple-element.20), calls=%async_computation.1 | async-start | bytes 16777216 | tf_op jit(solution)/shard_map/all_to_all | solution.py:44
  210.2 4.5 copy-start.3
  210.3 159.1 %all-gather.2.cloned.1.call-start = ((), (), s32[]{:S(2)}) async-start(), calls=%async_computation.7 | async-start | bytes 9437184 | tf_op jit(solution)/shard_map/all_gather | solution.py:73
  214.2 670.9 %reduce-scatter.2.cloned.1.call-start = ((), (), s32[]{:S(2)}) async-start(), calls=%async_computation.8 | async-start | bytes 28311552 | tf_op jit(solution)/shard_map/reduce_scatter | solution.py:101
  227.5 92.3 %copy-start.4 = (bf16[1,1,768,1536]{2,3,1,0:T(8,128)(2,1)S(1)}, bf16[1,1,768,1536]{2,3,1,0:T(8,128)(2,1)}, u32[]{:S(2)}) copy-start(bf16[1,1,768,1536]{2,3,1,0:T(8,128)(2,1)} %copy.30) | copy-start | bytes 7077892
  380.3 12.9 %copy-start.10 = (bf16[768,768]{0,1:T(8,128)(2,1)}, bf16[768,768]{0,1:T(8,128)(2,1)S(1)}, u32[]{:S(2)}) copy-start(bf16[768,768]{0,1:T(8,128)(2,1)S(1)} %get-tuple-element.14) | copy-start | bytes 3538948
  418.9 292.9 %copy-start.11 = (bf16[768,768]{0,1:T(8,128)(2,1)S(1)}, bf16[768,768]{0,1:T(8,128)(2,1)}, u32[]{:S(2)}) copy-start(bf16[768,768]{0,1:T(8,128)(2,1)} %copy-done.10) | copy-start | bytes 3538948
  418.9 293.0 %copy-start.12 = (bf16[768,768]{0,1:T(8,128)(2,1)S(1)}, bf16[768,768]{0,1:T(8,128)(2,1)}, u32[]{:S(2)}) copy-start(bf16[768,768]{0,1:T(8,128)(2,1)} %get-tuple-element.15) | copy-start | bytes 3538948
  418.9 281.3 %all-to-all-start.2 = ((bf16[2,2048,1536]{2,1,0:T(8,128)(2,1)}), bf16[2,2048,1536]{2,1,0:T(8,128)(2,1)}, u32[]{:S(2)}, u32[]{:S(2)}) async-start(bf16[2,2048,1536]{2,1,0:T(8,128)(2,1)} %pad_maximum_fusion.1), calls=%async_computation.2 | async-start | bytes 25165824 | tf_op jit(solution)/shard_map/all_to_all | solution.py:90
  700.2 36.5 %all-to-all-start.4 = ((bf16[64,1,12]{2,1,0:T(2,128)(2,1)}), bf16[64,1,12]{2,1,0:T(2,128)(2,1)S(1)}, u32[]{:S(2)}, u32[]{:S(2)}) async-start(bf16[64,1,12]{2,1,0:T(2,128)(2,1)} %convert_element_type.56), calls=%async_computation.4 | async-start | bytes 65536 | tf_op jit(solution)/shard_map/all_to_all | solution.py:115
  736.7 11.1 %copy-start.9 = (s32[1024,1]{0,1:T(1,128)S(1)}, s32[1024,1]{0,1:T(1,128)}, u32[]{:S(2)}) copy-start(s32[1024,1]{0,1:T(1,128)} %get-tuple-element.17) | copy-start | bytes 12292
  736.7 18.2 %copy-start.6 = (s32[128,8]{1,0:T(8,128)S(1)}, s32[128,8]{1,0:T(8,128)}, u32[]{:S(2)}) copy-start(s32[128,8]{1,0:T(8,128)} %copy-done.5) | copy-start | bytes 12292
  736.7 111.4 %all-to-all-start.3 = ((bf16[64,12,4096]{2,1,0:T(8,128)(2,1)}), bf16[64,12,4096]{2,1,0:T(8,128)(2,1)}, u32[]{:S(2)}, u32[]{:S(2)}) async-start(bf16[64,12,4096]{2,1,0:T(8,128)(2,1)} %reshape.175), calls=%async_computation.3 | async-start | bytes 16777216 | tf_op jit(solution)/shard_map/all_to_all | solution.py:108
  858.0 18.7 %copy-start.8 = (pred[128,8]{1,0:T(8,128)(4,1)S(1)}, pred[128,8]{1,0:T(8,128)(4,1)}, u32[]{:S(2)}) copy-start(pred[128,8]{1,0:T(8,128)(4,1)} %copy-done.7) | copy-start | bytes 3076
  885.2 12.7 %copy-start.1 = (bf16[128,4096]{1,0:T(8,128)(2,1)S(1)}, bf16[128,4096]{1,0:T(8,128)(2,1)}, u32[]{:S(2)}) copy-start(bf16[128,4096]{1,0:T(8,128)(2,1)} %param.6) | copy-start | bytes 3145732
Sparse Core Ops, SparseCore 0:
  214.3 154.9 all-gather.1
  410.3 441.0 reduce-scatter.1
